TPU v7x, 512 devices: a whole 4x8x8 slice. The times are simulated.
512 devices in a mesh: sub: 8 (over x, core), seq: 8 (over y), exp: 8 (over z).
Axes of the slice: x: 4, y: 8, z: 8, core: 2. Of those that a mesh axis runs over, the one named last changes fastest.
Arguments:
- node_features: bfloat16 [64, 1536, 1024], P(('sub', 'exp'), 'seq'), parts along dimension 0, may hold values from -24 to 24
- block_mask: int32 [64, 12, 12], P(('sub', 'exp')), parts along dimension 0, may hold values from 0 to 1, as said below
- w_qkv: bfloat16 [1024, 3072], P('exp', 'seq'), may hold values from -4 to 4
- w_out: bfloat16 [1024, 1024], P('seq', 'exp'), may hold values from -0.1875 to 0.1875
- norm_gain: float32 [1024], replicated, may hold values from 0.5 to 1.5
- routes: int32 [64, 1536, 2], P(('sub', 'exp'), 'seq'), parts along dimension 0, may hold values from 0 to 63, all different within a row; in each aligned block of 192 rows (0 to 191, 192 to 383, ..., all dimensions but the last counted through in order) at most 12 rows name the same one
- gates: float32 [64, 1536, 2], P(('sub', 'exp'), 'seq'), parts along dimension 0, may hold values from 0.1 to 1
- w_gate_up: bfloat16 [64, 1024, 1024], P(('seq', 'exp')), may hold values from -0.1875 to 0.1875
- w_down: bfloat16 [64, 512, 1024], P(('seq', 'exp')), may hold values from -0.25 to 0.25
Outputs:
- layer_out: bfloat16 [64, 1536, 1024], P(('sub', 'exp'), 'seq'), parts along dimension 0
There are 8 independent parts, one for each index of `sub`. A program takes and returns all parts, laid end to end along the dimension named above; an argument that names none is the same for every part. Nothing has to cross between parts.
Inputs may be any that keep to these rules, and one draw needn't show every extreme that they name: In each aligned block of 192 rows (one device's nodes, subgraphs then nodes in order) no expert is named by more than 12 of the rows' routes, a bound that some block reaches; the 2 experts of a node differ. `block_mask`: the diagonal blocks are 1.
All inputs are finite; a program needn't handle non-finite values.
Results may differ from a plain program's by a relative error of at most 0.0065.
The roundings to bfloat16 on the way count: a program that leaves them out, or rounds other values in their place, can miss the bound.
Values may be sent and summed in bfloat16 or wider, within the bound.
No kernel may reach another device: no remote copies, remote signals or barrier semaphores. Data moves between devices by JAX's collectives and lax.ppermute only.
A program may use at most 64 MiB of HBM per device.

v0:
```python
import math
import jax
import jax.numpy as jnp
from jax import lax
from jax.sharding import PartitionSpec as P

HEAD_DIM = 64
TOP = 2
BLOCK = 128


def per_device(
    node_features, block_mask, w_qkv, w_out, norm_gain, routes, gates, w_gate_up, w_down
):
    feats = node_features[0]
    node_dev, width = feats.shape
    seq_count = lax.axis_size("seq")
    exp_count = lax.axis_size("exp")
    experts = seq_count * exp_count * w_gate_up.shape[0]
    head_cols = w_qkv.shape[1]
    qkv_all, out_all = (
        lax.all_gather(w_qkv[None], ("seq", "exp"), axis=0, tiled=True),
        lax.all_gather(w_out[None], ("seq", "exp"), axis=0, tiled=True),
    )
    qkv_tiles = qkv_all.reshape(seq_count, exp_count, w_qkv.shape[0], head_cols)
    local_proj = jnp.einsum(
        "nek,sekc->nsc",
        feats.reshape(node_dev, exp_count, w_qkv.shape[0]),
        qkv_tiles,
        preferred_element_type=jnp.float32,
    )
    local_proj = local_proj.astype(jnp.bfloat16).reshape(node_dev, seq_count * head_cols)
    projected = lax.all_to_all(local_proj, "seq", split_axis=1, concat_axis=0, tiled=True)
    nodes = projected.shape[0]
    heads_here = head_cols // (3 * HEAD_DIM)
    split = projected.reshape(nodes, heads_here, 3, HEAD_DIM)
    query = split[:, :, 0]
    keys = split[:, :, 1]
    values = split[:, :, 2]
    col_mask = jnp.repeat(block_mask[0], BLOCK, axis=1) > 0
    span = math.gcd(nodes, 512)
    scale = 1.0 / math.sqrt(HEAD_DIM)

    def attend(index):
        start = index * span
        rows_query = lax.dynamic_slice_in_dim(query, start, span, 0)
        rows_mask = lax.dynamic_slice_in_dim(col_mask, start // BLOCK, span // BLOCK, 0)
        allowed = jnp.repeat(rows_mask, BLOCK, axis=0)
        scores = (
            jnp.einsum("qhd,khd->hqk", rows_query, keys, preferred_element_type=jnp.float32) * scale
        )
        scores = jnp.where(allowed[None], scores, -1e30)
        top = jnp.max(scores, axis=-1, keepdims=True)
        weights = jnp.exp(scores - top)
        probs = (weights / jnp.sum(weights, axis=-1, keepdims=True)).astype(jnp.bfloat16)
        return jnp.einsum("hqk,khd->qhd", probs, values, preferred_element_type=jnp.float32).astype(
            jnp.bfloat16
        )

    blocks = lax.map(attend, jnp.arange(nodes // span, dtype=jnp.int32))
    attended = blocks.reshape(nodes, heads_here * HEAD_DIM)
    node_attended = lax.all_to_all(attended, "seq", split_axis=0, concat_axis=1, tiled=True)
    out_tiles = out_all.reshape(seq_count, exp_count, w_out.shape[0], w_out.shape[1])
    attn_out = jnp.einsum(
        "nsk,sekc->nec",
        node_attended.reshape(node_dev, seq_count, w_out.shape[0]),
        out_tiles,
        preferred_element_type=jnp.float32,
    )
    mixed = feats.astype(jnp.float32) + attn_out.reshape(node_dev, width)
    mean_square = jnp.mean(mixed * mixed, axis=-1, keepdims=True)
    normed = (mixed * lax.rsqrt(mean_square + 1e-06) * norm_gain).astype(jnp.bfloat16)
    capacity = 2 * TOP * node_dev // experts
    pair_routes = routes[0].reshape(node_dev * TOP)
    onehot = (pair_routes[:, None] == jnp.arange(experts, dtype=jnp.int32)).astype(jnp.int32)
    earlier = jnp.cumsum(onehot, axis=0, dtype=jnp.int32) - onehot
    slots = jnp.sum(earlier * onehot, axis=1, dtype=jnp.int32)
    position = pair_routes * capacity + slots
    outgoing = (
        jnp.zeros((experts * capacity, width), jnp.bfloat16)
        .at[position]
        .set(jnp.repeat(normed, TOP, axis=0))
    )
    outgoing = outgoing.reshape(experts, capacity, width)
    hidden_units = w_down.shape[1]
    received = lax.all_to_all(outgoing, ("seq", "exp"), split_axis=0, concat_axis=0, tiled=True)
    sources, items, columns = received.shape
    flat_rows = received.reshape(sources * items, columns)
    both = jnp.dot(flat_rows, w_gate_up[0], preferred_element_type=jnp.float32)
    hidden = (jax.nn.silu(both[:, :hidden_units]) * both[:, hidden_units:]).astype(jnp.bfloat16)
    result = jnp.dot(hidden, w_down[0], preferred_element_type=jnp.float32).astype(jnp.bfloat16)
    processed = result.reshape(sources, items, columns)
    returned = lax.all_to_all(
        processed, ("seq", "exp"), split_axis=0, concat_axis=0, tiled=True
    ).reshape(experts * capacity, width)
    picked = returned[position].astype(jnp.float32).reshape(node_dev, TOP, width)
    expert_sum = jnp.sum(picked * gates[0][:, :, None], axis=1)
    return (mixed + expert_sum).astype(jnp.bfloat16)[None]


def solution(mesh):
    in_specs = (
        P(("sub", "exp"), "seq", None),
        P(("sub", "exp"), None, None),
        P("exp", "seq"),
        P("seq", "exp"),
        P(),
        P(("sub", "exp"), "seq", None),
        P(("sub", "exp"), "seq", None),
        P(("seq", "exp"), None, None),
        P(("seq", "exp"), None, None),
    )
    out_specs = P(("sub", "exp"), "seq", None)
    return jax.shard_map(
        per_device, mesh=mesh, in_specs=in_specs, out_specs=out_specs, check_vma=False
    )
```

profile of v0, /device:TPU:24, one launch (start us, length us, event | category | flops | bytes accessed | tf_op | source)
XLA Modules:
  0.0 382.8 jit_solution(14159090257780799350)
XLA Ops:
  6.5 0.0 copy-start
  6.5 0.0 all-gather.5.cloned.1.call-start
  6.5 0.7 all-gather.5.cloned.1.call-update
  7.3 1.1 copy.33
  8.3 97.1 %all-gather.5.cloned.1.call-done = bf16[8192,384]{1,0:T(8,128)(2,1)} async-done(((bf16[128,384]{1,0:T(8,128)(2,1)}), bf16[8192,384]{1,0:T(8,128)(2,1)}) %all-gather.5.cloned.1.call-update) | async-done | bytes 6291472 | tf_op jit(solution)/shard_map/all_gather | solution.py:22
  105.4 5.2 %bitcast_convert_fusion = bf16[192,8,384]{2,0,1:T(8,128)(2,1)} fusion(bf16[8,8,128,384]{3,2,1,0:T(8,128)(2,1)} %bitcast.99, bf16[192,8,128]{2,1,0:T(8,128)(2,1)S(1)} %bitcast.103), kind=kOutput, calls=%fused_computation.28 | convolution fusion | flops 1208549376 | bytes 7864320 | tf_op jit(solution)/shard_map/nek,sekc->nsc/dot_general | solution.py:26
  110.7 6.1 %all-to-all-start = ((bf16[192,8,384]{2,0,1:T(8,128)(2,1)}), bf16[192,8,384]{2,0,1:T(8,128)(2,1)S(1)}, u32[]{:S(2)}, u32[]{:S(2)}) async-start(bf16[192,8,384]{2,0,1:T(8,128)(2,1)} %bitcast_convert_fusion), calls=%async_computation | async-start | bytes 2359296 | tf_op jit(solution)/shard_map/all_to_all | solution.py:33
  116.7 0.0 all-gather.7.cloned.1.call-start
  116.7 0.7 all-gather.7.cloned.1.call-update
  117.5 0.0 copy-done.4
  117.5 0.1 copy.23
  117.6 0.1 eq.29
  117.7 0.1 eq.25
  117.9 0.0 copy-done.5
  117.9 0.1 broadcast_in_dim.65
  118.1 26.0 %all-to-all-done = bf16[192,8,384]{2,0,1:T(8,128)(2,1)S(1)} async-done(((bf16[192,8,384]{2,0,1:T(8,128)(2,1)}), bf16[192,8,384]{2,0,1:T(8,128)(2,1)S(1)}, u32[]{:S(2)}, u32[]{:S(2)}) %all-to-all-start) | async-done | bytes 1179680 | tf_op jit(solution)/shard_map/all_to_all | solution.py:33
  144.1 2.0 copy.18
  146.1 2.9 reshape.112
  149.0 1.1 slice_bitcast_fusion
  150.1 28.0 %while.12 = (s32[]{:T(128)}, bf16[3,512,2,64]{1,3,2,0:T(8,128)(2,1)}, s32[3]{0:T(128)S(1)}, pred[12,1536]{1,0:T(8,128)(4,1)S(1)}, bf16[1536,2,64]{0,2,1:T(8,128)...) while((s32[]{:T(128)}, ...), condition=%wide.region_3.4_spmd, body=%wide.region_0.3_spmd.sunk | while | flops 618205184 | bytes 5532574 | solution.py:60
  150.1 0.6 dynamic_slice.40
  151.3 0.2 broadcast_in_dim.104
  151.5 3.5 fusion.73
  155.0 4.4 %fusion.74 = bf16[3,512,2,64]{1,3,2,0:T(8,128)(2,1)} fusion(bf16[3,512,2,64]{1,3,2,0:T(8,128)(2,1)} %get-tuple-element.174, s32[]{:T(128)} %get-tuple-element.173, bf16[1536,2,64]{0,2,1:T(8,128)(2,1)S(1)} %copy-done.3, f32[2,512]{1,0:T(2,128)S(1)} %fusion.73, pred[512,1536]{1,0:T(8,128)(4,1)S(1)} %bitcast.97, ...), kind=kOutput, calls=%fused_computation.13.clone.1 | convolution fusion | flops 410585600 | bytes 1839620 | tf_op jit(solution)/shard_map/while/body/eval_jaxpr/hqk,khd->qhd/dot_general | solution.py:56
  159.4 0.6 dynamic_slice.40
  160.6 0.2 broadcast_in_dim.104
  160.9 0.0 copy-start.3
  160.9 3.5 fusion.73
  164.4 4.4 %fusion.74 = bf16[3,512,2,64]{1,3,2,0:T(8,128)(2,1)} fusion(bf16[3,512,2,64]{1,3,2,0:T(8,128)(2,1)} %get-tuple-element.174, s32[]{:T(128)} %get-tuple-element.173, bf16[1536,2,64]{0,2,1:T(8,128)(2,1)S(1)} %copy-done.3, f32[2,512]{1,0:T(2,128)S(1)} %fusion.73, pred[512,1536]{1,0:T(8,128)(4,1)S(1)} %bitcast.97, ...), kind=kOutput, calls=%fused_computation.13.clone.1 | convolution fusion | flops 410585600 | bytes 1839620 | tf_op jit(solution)/shard_map/while/body/eval_jaxpr/hqk,khd->qhd/dot_general | solution.py:56
  168.8 0.6 dynamic_slice.40
  170.0 0.2 broadcast_in_dim.104
  170.2 3.5 fusion.73
  173.7 4.4 %fusion.74 = bf16[3,512,2,64]{1,3,2,0:T(8,128)(2,1)} fusion(bf16[3,512,2,64]{1,3,2,0:T(8,128)(2,1)} %get-tuple-element.174, s32[]{:T(128)} %get-tuple-element.173, bf16[1536,2,64]{0,2,1:T(8,128)(2,1)S(1)} %copy-done.3, f32[2,512]{1,0:T(2,128)S(1)} %fusion.73, pred[512,1536]{1,0:T(8,128)(4,1)S(1)} %bitcast.97, ...), kind=kOutput, calls=%fused_computation.13.clone.1 | convolution fusion | flops 410585600 | bytes 1839620 | tf_op jit(solution)/shard_map/while/body/eval_jaxpr/hqk,khd->qhd/dot_general | solution.py:56
  178.1 2.2 copy.28
  180.3 1.1 reshape.145
  181.4 8.0 %all-to-all-start.1 = ((bf16[8,192,128]{2,1,0:T(8,128)(2,1)}), bf16[8,192,128]{2,1,0:T(8,128)(2,1)S(1)}, u32[]{:S(2)}, u32[]{:S(2)}) async-start(bf16[8,192,128]{2,1,0:T(8,128)(2,1)} %reshape.145), calls=%async_computation.1 | async-start | bytes 786432 | tf_op jit(solution)/shard_map/all_to_all | solution.py:62
  189.4 0.9 reduce-window.6
  190.3 0.2 slice_reduce_fusion
  190.6 0.1 copy.22
  190.7 0.1 mul.72
  190.9 0.1 fusion.48
  191.0 16.6 %all-gather.7.cloned.1.call-done = bf16[8192,128]{1,0:T(8,128)(2,1)} async-done(((bf16[128,128]{1,0:T(8,128)(2,1)}), bf16[8192,128]{1,0:T(8,128)(2,1)}) %all-gather.7.cloned.1.call-update) | async-done | bytes 2097168 | tf_op jit(solution)/shard_map/all_gather | solution.py:23
  207.6 4.0 %copy.21 = bf16[8,8,128,128]{2,3,1,0:T(8,128)(2,1)} copy(bf16[8,8,128,128]{3,2,1,0:T(8,128)(2,1)} %bitcast.101) | data formatting | bytes 4194304 | tf_op jit(solution)/shard_map/reshape | solution.py:63
  211.6 0.0 all-to-all-done.1
  211.6 0.7 copy-done.2
  212.3 2.7 multiply_reduce_fusion.1
  215.0 0.1 multiply_convert_fusion
  215.2 1.3 broadcast_in_dim.69
  216.5 3.0 reshape.134
  219.4 4.0 %scatter_custom_fusion = bf16[768,1024]{1,0:T(8,128)(2,1)} fusion(s32[384]{0:T(512)S(1)} %fusion.50, bf16[384,1024]{1,0:T(8,128)(2,1)} %reshape.134, bf16[]{:T(256)} %constant.96.clone.1), kind=kCustom, calls=%fused_computation.42 | custom fusion | bytes 1573376 | tf_op jit(solution)/shard_map/scatter | solution.py:82
  223.4 3.6 reshape.116
  227.0 59.8 %all_to_all.39 = bf16[64,12,1024]{2,1,0:T(8,128)(2,1)} all-to-all(bf16[64,12,1024]{2,1,0:T(8,128)(2,1)} %reshape.116), channel_id=1, replica_groups=mesh['sub'=8,'seq'=8,'exp'=8] {'seq','exp'}, dimensions={0} | all-to-all | bytes 3145728 | tf_op jit(solution)/shard_map/all_to_all | solution.py:86
  286.8 3.6 reshape.117
  290.4 3.3 fusion.33
  293.7 2.2 convolution_convert_fusion
  295.9 3.6 reshape.118
  299.5 7.7 %all-to-all-start.3 = ((bf16[64,12,1024]{2,1,0:T(8,128)(2,1)}), bf16[64,12,1024]{2,1,0:T(8,128)(2,1)}, u32[]{:S(2)}, u32[]{:S(2)}) async-start(bf16[64,12,1024]{2,1,0:T(8,128)(2,1)} %reshape.118), calls=%async_computation.3 | async-start | bytes 4194304 | tf_op jit(solution)/shard_map/all_to_all | solution.py:93
  307.2 0.1 copy.26
  307.3 52.9 %all-to-all-done.3 = bf16[64,12,1024]{2,1,0:T(8,128)(2,1)} async-done(((bf16[64,12,1024]{2,1,0:T(8,128)(2,1)}), bf16[64,12,1024]{2,1,0:T(8,128)(2,1)}, u32[]{:S(2)}, u32[]{:S(2)}) %all-to-all-start.3) | async-done | bytes 1572896 | tf_op jit(solution)/shard_map/all_to_all | solution.py:93
  360.2 3.6 reshape.119
  363.8 5.0 %gather_fusion = bf16[384,1024]{1,0:T(8,128)(2,1)} fusion(bf16[768,1024]{1,0:T(8,128)(2,1)} %reshape.119, s32[1024]{0:T(1024)S(1)} %pad_clamp_fusion), kind=kCustom, calls=%fused_computation | custom fusion | bytes 1574400 | tf_op jit(solution)/shard_map/gather | solution.py:96
  368.7 3.0 reshape.121
  371.7 3.4 multiply_reduce_fusion
  375.1 0.8 fusion.42
  (32 shorter events, 0.2 us)
Async XLA Ops:
  6.5 283.9 %copy-start = (bf16[1,1024,1024]{2,1,0:T(8,128)(2,1)S(1)}, bf16[1,1024,1024]{2,1,0:T(8,128)(2,1)}, u32[]{:S(2)}) copy-start(bf16[1,1024,1024]{2,1,0:T(8,128)(2,1)} %param.18) | copy-start | bytes 6291460
  6.5 98.9 %all-gather.5.cloned.1.call-start = ((), (), s32[]{:S(2)}) async-start(), calls=%async_computation.4 | async-start | bytes 6389760 | tf_op jit(solution)/shard_map/all_gather | solution.py:22
  110.7 6.8 %copy-start.4 = (s32[1,192,2]{1,2,0:T(2,128)S(1)}, s32[1,192,2]{1,2,0:T(2,128)}, u32[]{:S(2)}) copy-start(s32[1,192,2]{1,2,0:T(2,128)} %param.16) | copy-start | bytes 4612
  110.7 7.2 %copy-start.5 = (s32[1,12,12]{2,0,1:T(1,128)S(1)}, s32[1,12,12]{2,0,1:T(1,128)}, u32[]{:S(2)}) copy-start(s32[1,12,12]{2,0,1:T(1,128)} %param.12) | copy-start | bytes 1732
  110.7 33.4 %all-to-all-start = ((bf16[192,8,384]{2,0,1:T(8,128)(2,1)}), bf16[192,8,384]{2,0,1:T(8,128)(2,1)S(1)}, u32[]{:S(2)}, u32[]{:S(2)}) async-start(bf16[192,8,384]{2,0,1:T(8,128)(2,1)} %bitcast_convert_fusion), calls=%async_computation | async-start | bytes 2359296 | tf_op jit(solution)/shard_map/all_to_all | solution.py:33
  116.7 90.9 %all-gather.7.cloned.1.call-start = ((), (), s32[]{:S(2)}) async-start(), calls=%async_computation.5 | async-start | bytes 2129920 | tf_op jit(solution)/shard_map/all_gather | solution.py:23
  151.5 3.5 copy-start.3
  160.9 3.5 copy-start.3
  170.2 3.5 copy-start.3
  181.4 30.2 %all-to-all-start.1 = ((bf16[8,192,128]{2,1,0:T(8,128)(2,1)}), bf16[8,192,128]{2,1,0:T(8,128)(2,1)S(1)}, u32[]{:S(2)}, u32[]{:S(2)}) async-start(bf16[8,192,128]{2,1,0:T(8,128)(2,1)} %reshape.145), calls=%async_computation.1 | async-start | bytes 786432 | tf_op jit(solution)/shard_map/all_to_all | solution.py:62
  207.6 4.7 %copy-start.1 = (bf16[1,192,1024]{2,1,0:T(8,128)(2,1)S(1)}, bf16[1,192,1024]{2,1,0:T(8,128)(2,1)}, u32[]{:S(2)}) copy-start(bf16[1,192,1024]{2,1,0:T(8,128)(2,1)} %param.11) | copy-start | bytes 1179652
  211.6 3.4 copy-start.6
  211.6 0.7 copy-start.2
  290.4 3.3 copy-start.8
  299.5 7.7 %copy-start.7 = (f32[1,192,2]{1,2,0:T(2,128)S(1)}, f32[1,192,2]{1,2,0:T(2,128)}, u32[]{:S(2)}) copy-start(f32[1,192,2]{1,2,0:T(2,128)} %param.17) | copy-start | bytes 4612
  299.5 60.7 %all-to-all-start.3 = ((bf16[64,12,1024]{2,1,0:T(8,128)(2,1)}), bf16[64,12,1024]{2,1,0:T(8,128)(2,1)}, u32[]{:S(2)}, u32[]{:S(2)}) async-start(bf16[64,12,1024]{2,1,0:T(8,128)(2,1)} %reshape.118), calls=%async_computation.3 | async-start | bytes 4194304 | tf_op jit(solution)/shard_map/all_to_all | solution.py:93
Sparse Core Ops, SparseCore 0:
  10.4 94.9 all-gather.4
  120.6 86.9 all-gather.6
where the time goes:
time: 384 us; the launch traced here: 383 us
  waiting for transfers between devices  194 us (51%)
  blocking collectives  59.8 us (16%)
  local copies, waits for them, and re-layouts  49.3 us (13%)
  matrix products  37 us (10%)
  starting transfers between devices  21.8 us (6%)
  between operations  13.6 us (4%)
  other arithmetic  5.53 us (1%)
    all_gather x1, waiting for transfers between devices, per_device(): lax.all_gather(w_qkv[None], ('seq', 'exp'), axis=0, tiled=True)  97.1 us
    all_to_all x1, blocking collectives, per_device(): lax.all_to_all(outgoing, ('seq', 'exp'), split_axis=0, concat_axis=0, til...  59.8 us
    all_to_all x1, waiting for transfers between devices, per_device(): lax.all_to_all(processed, ('seq', 'exp'), split_axis=0, concat_axis=0, ti...  52.9 us
    all_to_all x1, waiting for transfers between devices, per_device(): lax.all_to_all(local_proj, 'seq', split_axis=1, concat_axis=0, tiled=True)  26 us
    all_gather x1, waiting for transfers between devices, per_device(): lax.all_gather(w_out[None], ('seq', 'exp'), axis=0, tiled=True)  16.6 us
    dot_general x3, matrix products, attend(): jnp.einsum('hqk,khd->qhd', probs, values, preferred_element_type=jnp.floa...  13.2 us
    sub x3, matrix products, attend(): weights = jnp.exp(scores - top)  10.4 us
    all_to_all x1, starting transfers between devices, per_device(): lax.all_to_all(attended, 'seq', split_axis=0, concat_axis=1, tiled=True)  8.03 us
  transfers between devices with their start and end apart: 5, of which 4 were waited for; matrix products, arithmetic and copies ran while one was open for 11% of the time, Pallas kernels for 0%

commit v1 on v0

--- a/solution.py
+++ b/solution.py
@@ -1,3 +1,4 @@
+import functools
 import math
 import jax
 import jax.numpy as jnp
@@ -7,6 +8,20 @@
 HEAD_DIM = 64
 TOP = 2
 BLOCK = 128
+
+
+def object_write(array_in, axis_tag):
+    workers = lax.axis_size(axis_tag)
+    block_list = []
+    for j in [*range(array_in.ndim)]:
+        block_list.append(workers if j == 0 else 1)
+    k_now = lax.all_to_all(
+        jnp.tile(array_in, block_list), axis_tag, split_axis=0, concat_axis=0, tiled=True
+    )
+    return k_now
+
+
+play_state = functools.partial(object_write, axis_tag=("seq", "exp"))
 
 
 def per_device(
@@ -19,7 +34,7 @@
     experts = seq_count * exp_count * w_gate_up.shape[0]
     head_cols = w_qkv.shape[1]
     qkv_all, out_all = (
-        lax.all_gather(w_qkv[None], ("seq", "exp"), axis=0, tiled=True),
+        play_state(w_qkv[None]),
         lax.all_gather(w_out[None], ("seq", "exp"), axis=0, tiled=True),
     )
     qkv_tiles = qkv_all.reshape(seq_count, exp_count, w_qkv.shape[0], head_cols)

time: 384 us -> 539 us (1.40)
  the two profiles are of different devices: /device:TPU:24 before, /device:TPU:30 now
where the time goes in v1:
time: 539 us; the launch traced here: 537 us
  waiting for transfers between devices  306 us (57%)
  blocking collectives  61.3 us (11%)
  starting transfers between devices  59.1 us (11%)
  local copies, waits for them, and re-layouts  53 us (10%)
  matrix products  37 us (7%)
  between operations  13.6 us (3%)
  other arithmetic  5.53 us (1%)
    all_to_all x1, waiting for transfers between devices, object_write(): lax.all_to_all(jnp.tile(array_in, block_list), axis_tag, split_axis=0, co...  202 us
    all_to_all x1, blocking collectives, per_device(): lax.all_to_all(outgoing, ('seq', 'exp'), split_axis=0, concat_axis=0, til...  61.3 us
    all_to_all x1, waiting for transfers between devices, per_device(): lax.all_to_all(processed, ('seq', 'exp'), split_axis=0, concat_axis=0, ti...  51.5 us
    all_to_all x1, starting transfers between devices, per_device(): lax.all_to_all(local_proj, 'seq', split_axis=1, concat_axis=0, tiled=True)  26.6 us
    all_gather x1, waiting for transfers between devices, per_device(): lax.all_gather(w_out[None], ('seq', 'exp'), axis=0, tiled=True)  26.6 us
    all_to_all x1, waiting for transfers between devices, per_device(): lax.all_to_all(local_proj, 'seq', split_axis=1, concat_axis=0, tiled=True)  24.6 us
    all_to_all x1, starting transfers between devices, object_write(): lax.all_to_all(jnp.tile(array_in, block_list), axis_tag, split_axis=0, co...  16.7 us
    dot_general x3, matrix products, attend(): jnp.einsum('hqk,khd->qhd', probs, values, preferred_element_type=jnp.floa...  13.2 us
  transfers between devices with their start and end apart: 5, of which 4 were waited for; matrix products, arithmetic and copies ran while one was open for 8% of the time, Pallas kernels for 0%

profile of v1, /device:TPU:30, one launch (start us, length us, event | category | flops | bytes accessed | tf_op | source)
XLA Modules:
  0.0 537.1 jit_solution(10195134929377699106)
XLA Ops:
  6.5 0.0 copy-start
  6.5 4.7 tile.2
  11.2 16.7 %all-to-all-start = ((bf16[64,128,384]{2,1,0:T(8,128)(2,1)}), bf16[64,128,384]{2,1,0:T(8,128)(2,1)}, u32[]{:S(2)}, u32[]{:S(2)}) async-start(bf16[64,128,384]{2,1,0:T(8,128)(2,1)} %tile.2), calls=%async_computation | async-start | bytes 12582912 | tf_op jit(solution)/shard_map/all_to_all | solution.py:18
  28.0 0.0 copy-done.1
  28.0 0.1 copy.33
  28.0 202.4 %all-to-all-done = bf16[64,128,384]{2,1,0:T(8,128)(2,1)} async-done(((bf16[64,128,384]{2,1,0:T(8,128)(2,1)}), bf16[64,128,384]{2,1,0:T(8,128)(2,1)}, u32[]{:S(2)}, u32[]{:S(2)}) %all-to-all-start) | async-done | bytes 6291488 | tf_op jit(solution)/shard_map/all_to_all | solution.py:18
  230.5 5.2 bitcast_convert_fusion
  235.7 26.6 %all-to-all-start.1 = ((bf16[192,8,384]{2,0,1:T(8,128)(2,1)}), bf16[192,8,384]{2,0,1:T(8,128)(2,1)S(1)}, u32[]{:S(2)}, u32[]{:S(2)}) async-start(bf16[192,8,384]{2,0,1:T(8,128)(2,1)} %bitcast_convert_fusion), calls=%async_computation.1 | async-start | bytes 2359296 | tf_op jit(solution)/shard_map/all_to_all | solution.py:48
  262.3 0.0 all-gather.3.cloned.1.call-start
  262.3 0.7 all-gather.3.cloned.1.call-update
  263.1 0.1 copy.23
  263.2 0.1 eq.29
  263.3 0.1 eq.25
  263.5 0.1 broadcast_in_dim.62
  263.7 24.6 %all-to-all-done.1 = bf16[192,8,384]{2,0,1:T(8,128)(2,1)S(1)} async-done(((bf16[192,8,384]{2,0,1:T(8,128)(2,1)}), bf16[192,8,384]{2,0,1:T(8,128)(2,1)S(1)}, u32[]{:S(2)}, u32[]{:S(2)}) %all-to-all-start.1) | async-done | bytes 1179680 | tf_op jit(solution)/shard_map/all_to_all | solution.py:48
  288.2 2.0 copy.18
  290.3 2.9 reshape.115
  293.2 1.1 slice_bitcast_fusion
  294.2 28.0 %while.12 = (s32[]{:T(128)}, bf16[3,512,2,64]{1,3,2,0:T(8,128)(2,1)}, s32[3]{0:T(128)S(1)}, pred[12,1536]{1,0:T(8,128)(4,1)S(1)}, bf16[1536,2,64]{0,2,1:T(8,128)...) while((s32[]{:T(128)}, ...), condition=%wide.region_3.4_spmd, body=%wide.region_0.3_spmd.sunk | while | flops 618205184 | bytes 5532574 | solution.py:75
  294.2 0.6 dynamic_slice.40
  295.4 0.2 broadcast_in_dim.100
  295.7 3.5 fusion.73
  299.1 4.4 fusion.74
  303.6 0.6 dynamic_slice.40
  304.8 0.2 broadcast_in_dim.100
  305.0 3.5 fusion.73
  308.5 0.0 copy-done.4
  308.5 4.4 fusion.74
  312.9 0.6 dynamic_slice.40
  314.1 0.2 broadcast_in_dim.100
  314.3 3.5 fusion.73
  317.8 4.4 fusion.74
  322.2 2.2 copy.28
  324.4 1.1 reshape.146
  325.5 6.7 %all-to-all-start.2 = ((bf16[8,192,128]{2,1,0:T(8,128)(2,1)}), bf16[8,192,128]{2,1,0:T(8,128)(2,1)S(1)}, u32[]{:S(2)}, u32[]{:S(2)}) async-start(bf16[8,192,128]{2,1,0:T(8,128)(2,1)} %reshape.146), calls=%async_computation.2 | async-start | bytes 786432 | tf_op jit(solution)/shard_map/all_to_all | solution.py:77
  332.2 0.9 reduce-window.6
  333.1 0.2 slice_reduce_fusion
  333.4 0.1 copy.22
  333.5 0.1 mul.72
  333.6 0.1 fusion.48
  333.8 26.6 %all-gather.3.cloned.1.call-done = bf16[8192,128]{1,0:T(8,128)(2,1)} async-done(((bf16[128,128]{1,0:T(8,128)(2,1)}), bf16[8192,128]{1,0:T(8,128)(2,1)}) %all-gather.3.cloned.1.call-update) | async-done | bytes 2097168 | tf_op jit(solution)/shard_map/all_gather | solution.py:38
  360.4 4.0 copy.21
  364.4 0.0 all-to-all-done.2
  364.4 0.7 copy-done.3
  365.1 2.7 multiply_reduce_fusion.1
  367.8 0.1 multiply_convert_fusion
  368.0 1.3 broadcast_in_dim.65
  369.3 3.0 reshape.137
  372.2 4.0 scatter_custom_fusion
  376.2 3.6 reshape.119
  379.8 61.3 %all_to_all.44 = bf16[64,12,1024]{2,1,0:T(8,128)(2,1)} all-to-all(bf16[64,12,1024]{2,1,0:T(8,128)(2,1)} %reshape.119), channel_id=1, replica_groups=mesh['sub'=8,'seq'=8,'exp'=8] {'seq','exp'}, dimensions={0} | all-to-all | bytes 3145728 | tf_op jit(solution)/shard_map/all_to_all | solution.py:101
  441.1 3.6 reshape.120
  444.7 0.0 copy-done
  444.7 3.3 fusion.33
  448.0 2.2 convolution_convert_fusion
  450.2 3.6 reshape.121
  453.8 9.1 %all-to-all-start.4 = ((bf16[64,12,1024]{2,1,0:T(8,128)(2,1)}), bf16[64,12,1024]{2,1,0:T(8,128)(2,1)}, u32[]{:S(2)}, u32[]{:S(2)}) async-start(bf16[64,12,1024]{2,1,0:T(8,128)(2,1)} %reshape.121), calls=%async_computation.4 | async-start | bytes 4194304 | tf_op jit(solution)/shard_map/all_to_all | solution.py:108
  462.9 0.1 copy.26
  463.0 51.5 %all-to-all-done.4 = bf16[64,12,1024]{2,1,0:T(8,128)(2,1)} async-done(((bf16[64,12,1024]{2,1,0:T(8,128)(2,1)}), bf16[64,12,1024]{2,1,0:T(8,128)(2,1)}, u32[]{:S(2)}, u32[]{:S(2)}) %all-to-all-start.4) | async-done | bytes 1572896 | tf_op jit(solution)/shard_map/all_to_all | solution.py:108
  514.5 3.6 reshape.122
  518.1 5.0 gather_fusion
  523.1 3.0 reshape.124
  526.0 3.4 multiply_reduce_fusion
  529.5 0.8 fusion.42
  (34 shorter events, 0.2 us)
Async XLA Ops:
  6.5 438.2 %copy-start = (bf16[1,1024,1024]{2,1,0:T(8,128)(2,1)S(1)}, bf16[1,1024,1024]{2,1,0:T(8,128)(2,1)}, u32[]{:S(2)}) copy-start(bf16[1,1024,1024]{2,1,0:T(8,128)(2,1)} %param.18) | copy-start | bytes 6291460
  11.2 16.7 %copy-start.1 = (bf16[1,192,1024]{2,1,0:T(8,128)(2,1)S(1)}, bf16[1,192,1024]{2,1,0:T(8,128)(2,1)}, u32[]{:S(2)}) copy-start(bf16[1,192,1024]{2,1,0:T(8,128)(2,1)} %param.11) | copy-start | bytes 1179652
  11.2 219.2 %all-to-all-start = ((bf16[64,128,384]{2,1,0:T(8,128)(2,1)}), bf16[64,128,384]{2,1,0:T(8,128)(2,1)}, u32[]{:S(2)}, u32[]{:S(2)}) async-start(bf16[64,128,384]{2,1,0:T(8,128)(2,1)} %tile.2), calls=%async_computation | async-start | bytes 12582912 | tf_op jit(solution)/shard_map/all_to_all | solution.py:18
  235.7 27.4 %copy-start.5 = (s32[1,192,2]{1,2,0:T(2,128)S(1)}, s32[1,192,2]{1,2,0:T(2,128)}, u32[]{:S(2)}) copy-start(s32[1,192,2]{1,2,0:T(2,128)} %param.16) | copy-start | bytes 4612
  235.7 27.8 %copy-start.6 = (s32[1,12,12]{2,0,1:T(1,128)S(1)}, s32[1,12,12]{2,0,1:T(1,128)}, u32[]{:S(2)}) copy-start(s32[1,12,12]{2,0,1:T(1,128)} %param.12) | copy-start | bytes 1732
  235.7 52.5 %all-to-all-start.1 = ((bf16[192,8,384]{2,0,1:T(8,128)(2,1)}), bf16[192,8,384]{2,0,1:T(8,128)(2,1)S(1)}, u32[]{:S(2)}, u32[]{:S(2)}) async-start(bf16[192,8,384]{2,0,1:T(8,128)(2,1)} %bitcast_convert_fusion), calls=%async_computation.1 | async-start | bytes 2359296 | tf_op jit(solution)/shard_map/all_to_all | solution.py:48
  262.3 98.1 %all-gather.3.cloned.1.call-start = ((), (), s32[]{:S(2)}) async-start(), calls=%async_computation.5 | async-start | bytes 2129920 | tf_op jit(solution)/shard_map/all_gather | solution.py:38
  295.7 3.5 copy-start.4
  305.0 3.5 copy-start.4
  314.3 3.5 copy-start.4
  325.5 38.9 %all-to-all-start.2 = ((bf16[8,192,128]{2,1,0:T(8,128)(2,1)}), bf16[8,192,128]{2,1,0:T(8,128)(2,1)S(1)}, u32[]{:S(2)}, u32[]{:S(2)}) async-start(bf16[8,192,128]{2,1,0:T(8,128)(2,1)} %reshape.146), calls=%async_computation.2 | async-start | bytes 786432 | tf_op jit(solution)/shard_map/all_to_all | solution.py:77
  360.4 4.7 copy-start.2
  364.4 3.4 copy-start.7
  364.4 0.7 copy-start.3
  444.7 3.3 copy-start.9
  453.8 9.1 %copy-start.8 = (f32[1,192,2]{1,2,0:T(2,128)S(1)}, f32[1,192,2]{1,2,0:T(2,128)}, u32[]{:S(2)}) copy-start(f32[1,192,2]{1,2,0:T(2,128)} %param.17) | copy-start | bytes 4612
  453.8 60.7 %all-to-all-start.4 = ((bf16[64,12,1024]{2,1,0:T(8,128)(2,1)}), bf16[64,12,1024]{2,1,0:T(8,128)(2,1)}, u32[]{:S(2)}, u32[]{:S(2)}) async-start(bf16[64,12,1024]{2,1,0:T(8,128)(2,1)} %reshape.121), calls=%async_computation.4 | async-start | bytes 4194304 | tf_op jit(solution)/shard_map/all_to_all | solution.py:108
Sparse Core Ops, SparseCore 0:
  266.2 94.1 all-gather.2
